TPU v7x, 512 devices: a whole 4x8x8 slice. The times are simulated.
512 devices in a mesh: dp: 16 (over y, x_lo), table: 32 (over z, x_hi, core).
Axes of the slice: x: 4 (x_hi: 2, x_lo: 2; x = x_hi * 2 + x_lo), y: 8, z: 8, core: 2. Of those that a mesh axis runs over, the one named last changes fastest.
Arguments:
- id_table: bfloat16 [32768, 256], P('table'), may hold values from -2 to 2
- lookup_ids: int32 [65536, 8, 2], P(('dp', 'table')), may hold values from 0 to 32767, as said below
- row_owner: int32 [32768], replicated, may hold values from 0 to 32767, as said below
- query_tower: bfloat16 [1024, 256], replicated, may hold values from -1 to 1
- item_tower: bfloat16 [1024, 256], replicated, may hold values from -1 to 1
- row_seeds: int32 [32768], P('table'), may hold values from 0 to 1073741823
- tower_seeds: int32 [2, 1024], replicated, may hold values from 0 to 1073741823
Outputs:
- table_update: float32 [32768, 256], P('table')
- tower_update: float32 [2, 1024, 256], replicated
Inputs may be any that keep to these rules, and one draw needn't show every extreme that they name: `lookup_ids`: in every aligned block of 128 examples (the examples of one device), at most 96 of the lookups have row_owner[id] // 1024 equal to any one table shard, and exactly 96 do for some shard. A permutation: the row of id i lies at position row_owner[i] of id_table, on table shard row_owner[i] // 1024.
All inputs are finite; a program needn't handle non-finite values.
Results may differ from a plain program's by a relative error of at most 0.0073.
The roundings to bfloat16 on the way count: a program that leaves them out, or rounds other values in their place, can miss the bound.
Values may be sent and summed in bfloat16 or wider, within the bound.
No kernel may reach another device: no remote copies, remote signals or barrier semaphores. Data moves between devices by JAX's collectives and lax.ppermute only.
A program may use at most 64 MiB of HBM per device.

v0:
```python
import math
import jax
import jax.numpy as jnp
from jax import lax
from jax.sharding import PartitionSpec as P

NOISE_MULT = 0.1


def hashed_noise(seed_rows, width):
    columns = jnp.arange(width, dtype=jnp.int32)
    summed = jnp.zeros(seed_rows.shape + (width,), jnp.float32)
    for section in range(2):
        mixed = seed_rows[..., None] + (columns * 2 + section) * 1013904223
        mixed = mixed ^ mixed >> 15 & 131071
        mixed = mixed * 73244475
        mixed = mixed ^ mixed >> 13 & 524287
        mixed = mixed * 1597334677
        mixed = mixed ^ mixed >> 16 & 65535
        lower = (mixed & 65535).astype(jnp.float32) / 65536.0 - 0.5
        upper = (mixed >> 16 & 65535).astype(jnp.float32) / 65536.0 - 0.5
        summed = summed + lower + upper
    return summed * math.sqrt(3.0)


def squares(values):
    return jnp.sum(jnp.square(values.astype(jnp.float32)), axis=1)


def body(id_table, lookup_ids, row_owner, query_tower, item_tower, row_seeds, tower_seeds):
    shards = lax.axis_size("table")
    rows_dev, emb_width = id_table.shape
    batch, slots, bags = lookup_ids.shape
    feats = slots // 2
    hidden_width, out_width = query_tower.shape
    scale = 200.0 / math.sqrt(out_width)
    clip_norm = 0.9 * math.sqrt(2.0 * hidden_width + 400.0)
    requests = batch * slots * bags
    capacity = 3 * requests // (2 * shards)
    positions = row_owner[lookup_ids.reshape(-1)]
    owners = positions // rows_dev
    local_rows = positions - owners * rows_dev
    one_hot = (owners[:, None] == jnp.arange(shards, dtype=jnp.int32)[None, :]).astype(jnp.int32)
    ranks = jnp.sum((jnp.cumsum(one_hot, axis=0) - one_hot) * one_hot, axis=1)
    targets = owners * capacity + ranks
    outgoing = jnp.full((shards * capacity,), -1, jnp.int32).at[targets].set(local_rows)
    outgoing = outgoing.reshape(shards, capacity)
    incoming = lax.all_to_all(outgoing, "table", split_axis=0, concat_axis=0, tiled=True)
    valid = incoming >= 0
    fetched = id_table[jnp.where(valid, incoming, 0)]
    fetched = jnp.where(valid[:, :, None], fetched, jnp.zeros((), jnp.bfloat16))
    returned = lax.all_to_all(fetched, "table", split_axis=0, concat_axis=0, tiled=True)
    returned, incoming = (returned, incoming)
    looked = returned.reshape(shards * capacity, emb_width)[targets]
    pooled = jnp.sum(looked.reshape(batch, slots, bags, emb_width).astype(jnp.float32), axis=2)
    pooled = pooled.astype(jnp.bfloat16)
    query_in = pooled[:, :feats].reshape(batch, hidden_width)
    item_in = pooled[:, feats:].reshape(batch, hidden_width)
    query_vec = jnp.dot(query_in, query_tower, preferred_element_type=jnp.float32).astype(
        jnp.bfloat16
    )
    item_vec = jnp.dot(item_in, item_tower, preferred_element_type=jnp.float32).astype(jnp.bfloat16)
    all_items = lax.all_gather(item_vec, "dp", axis=0, tiled=True)
    scores = scale * lax.dot_general(
        query_vec, all_items, (((1,), (1,)), ((), ())), preferred_element_type=jnp.float32
    )
    peak = jnp.max(scores, axis=1, keepdims=True)
    log_total = peak + jnp.log(jnp.sum(jnp.exp(scores - peak), axis=1, keepdims=True))
    probs = jnp.exp(scores - log_total).astype(jnp.bfloat16)
    query_grad = (
        scale
        * (
            jnp.dot(probs, all_items, preferred_element_type=jnp.float32)
            - item_vec.astype(jnp.float32)
        )
    ).astype(jnp.bfloat16)
    weighted = lax.psum_scatter(
        lax.dot_general(
            probs, query_vec, (((0,), (0,)), ((), ())), preferred_element_type=jnp.float32
        ),
        "dp",
        scatter_dimension=0,
        tiled=True,
    )
    item_grad = (scale * (weighted - query_vec.astype(jnp.float32))).astype(jnp.bfloat16)
    query_back = lax.dot_general(
        query_grad, query_tower, (((1,), (1,)), ((), ())), preferred_element_type=jnp.float32
    )
    item_back = lax.dot_general(
        item_grad, item_tower, (((1,), (1,)), ((), ())), preferred_element_type=jnp.float32
    )
    norm_sq = (
        squares(query_in) * squares(query_grad)
        + squares(item_in) * squares(item_grad)
        + squares(query_back)
        + squares(item_back)
    )
    factor = jnp.minimum(1.0, clip_norm / jnp.sqrt(norm_sq + 1e-06))
    clipped_query = (factor[:, None] * query_grad.astype(jnp.float32)).astype(jnp.bfloat16)
    clipped_item = (factor[:, None] * item_grad.astype(jnp.float32)).astype(jnp.bfloat16)
    tower_part = jnp.stack(
        [
            lax.dot_general(
                query_in,
                clipped_query,
                (((0,), (0,)), ((), ())),
                preferred_element_type=jnp.float32,
            ),
            lax.dot_general(
                item_in, clipped_item, (((0,), (0,)), ((), ())), preferred_element_type=jnp.float32
            ),
        ]
    )
    tower_sum = lax.psum(tower_part, ("dp", "table"))
    back_all = jnp.concatenate(
        [query_back.reshape(batch, feats, emb_width), item_back.reshape(batch, feats, emb_width)],
        axis=1,
    )
    lookup_grad = (factor[:, None, None] * back_all).astype(jnp.bfloat16)
    spread = jnp.broadcast_to(lookup_grad[:, :, None, :], (batch, slots, bags, emb_width))
    spread = spread.reshape(requests, emb_width)
    grad_out = jnp.zeros((shards * capacity, emb_width), jnp.bfloat16).at[targets].set(spread)
    grad_in = lax.all_to_all(
        grad_out.reshape(shards, capacity, emb_width),
        "table",
        split_axis=0,
        concat_axis=0,
        tiled=True,
    )
    flat_in = incoming.reshape(-1)
    slot_rows = jnp.where(flat_in >= 0, flat_in, rows_dev)
    row_sum = (
        jnp.zeros((rows_dev, emb_width), jnp.float32)
        .at[slot_rows]
        .add(grad_in.reshape(shards * capacity, emb_width).astype(jnp.float32), mode="drop")
    )
    row_count = (
        jnp.zeros((rows_dev,), jnp.float32)
        .at[slot_rows]
        .add((flat_in >= 0).astype(jnp.float32), mode="drop")
    )
    row_sum, row_count = lax.psum((row_sum, row_count), "dp")
    row_noise = hashed_noise(row_seeds, emb_width)
    table_update = row_sum / clip_norm + NOISE_MULT * jnp.where(
        row_count[:, None] > 0.0, row_noise, 0.0
    )
    tower_update = tower_sum / clip_norm + NOISE_MULT * hashed_noise(tower_seeds, out_width)
    return (table_update, tower_update)


def solution(mesh):
    in_specs = (P("table", None), P(("dp", "table"), None, None), P(), P(), P(), P("table"), P())
    out_specs = (P("table", None), P())
    return jax.shard_map(body, mesh=mesh, in_specs=in_specs, out_specs=out_specs, check_vma=False)
```

profile of v0, /device:TPU:4, one launch (start us, length us, event | category | flops | bytes accessed | tf_op | source)
XLA Modules:
  0.0 749.2 jit_solution(12677365749732896167)
XLA Ops:
  7.2 1.0 copy.37
  8.6 11.8 %gather_fusion = s32[2048]{0:T(1024)S(1)} fusion(s32[32768]{0:T(1024)S(1)} %copy-done.1, s32[2048]{0:T(1024)S(1)} %broadcast_clamp_fusion.2), kind=kCustom, calls=%fused_computation | custom fusion | bytes 24576 | tf_op jit(solution)/shard_map/gather | solution.py:40
  20.4 9.1 %reduce-window.6 = s32[32,16,128]{2,1,0:T(8,128)S(1)} reduce-window(s32[32,16,128]{2,1,0:T(8,128)S(1)} %fusion.35, s32[]{:T(128)} %constant.35.clone.1), window={size=1x1x128 pad=0_0x0_0x127_0}, to_apply=%region_0.1 | reduce-window | flops 8323072 | bytes 524292 | tf_op jit(solution)/shard_map/reduce-window
  30.4 8.1 %scatter_custom_fusion = s32[3072]{0:T(1024)S(1)} fusion(s32[2048]{0:T(1024)S(1)} %bitcast.90, s32[2048]{0:T(1024)S(1)} %get-tuple-element.8, s32[]{:T(128)} %constant.34.clone.1), kind=kCustom, calls=%fused_computation.112 | custom fusion | bytes 12292 | tf_op jit(solution)/shard_map/scatter | solution.py:46
  38.6 20.4 %all_to_all.22 = s32[32,1,96]{2,1,0:T(1,128)S(1)} all-to-all(s32[32,1,96]{2,1,0:T(1,128)S(1)} %all_to_all.14), channel_id=1, replica_groups=mesh['dp'=16,'table'=32] {'table'}, dimensions={0} | all-to-all | bytes 24576 | tf_op jit(solution)/shard_map/all_to_all | solution.py:48
  59.7 11.1 %gather_fusion.1 = bf16[3072,256]{1,0:T(8,128)(2,1)S(1)} fusion(bf16[1024,256]{1,0:T(8,128)(2,1)S(1)} %copy-done, s32[3072]{0:T(1024)S(1)} %broadcast_clamp_fusion), kind=kCustom, calls=%fused_computation.1 | custom fusion | bytes 3158016 | tf_op jit(solution)/shard_map/gather | solution.py:50
  70.7 1.5 broadcast_select_fusion
  72.2 6.4 all-to-all-start.1
  78.7 39.2 %all-to-all-done.1 = bf16[32,96,256]{2,1,0:T(8,128)(2,1)S(1)} async-done(((bf16[32,96,256]{2,1,0:T(8,128)(2,1)}), bf16[32,96,256]{2,1,0:T(8,128)(2,1)S(1)}, u32[]{:S(2)}, u32[]{:S(2)}) %all-to-all-start.1) | async-done | bytes 1572896 | tf_op jit(solution)/shard_map/all_to_all | solution.py:52
  117.9 7.5 gather_fusion.2
  125.9 2.8 reduce_sum.88
  129.2 0.9 convolution_convert_fusion
  130.8 67.7 %all-gather.2.cloned.1.call-done = bf16[2048,256]{1,0:T(8,128)(2,1)} async-done(((bf16[128,256]{1,0:T(8,128)(2,1)}), bf16[2048,256]{1,0:T(8,128)(2,1)}) %all-gather.2.cloned.1.call-update) | async-done | bytes 1048592 | tf_op jit(solution)/shard_map/all_gather | solution.py:63
  198.5 1.8 fusion.56
  200.6 1.9 fusion.53
  202.6 1.8 multiply_reduce_fusion.2
  204.4 1.8 fusion.36
  206.9 73.6 %reduce-scatter.2.cloned.1.call-done = f32[128,256]{1,0:T(8,128)} async-done(((f32[2048,256]{1,0:T(8,128)}), f32[128,256]{1,0:T(8,128)}) %reduce-scatter.2.cloned.1.call-update) | async-done | bytes 131088 | tf_op jit(solution)/shard_map/reduce_scatter | solution.py:77
  280.5 1.0 fusion.38
  282.5 0.7 broadcast_in_dim.40
  283.7 10.7 %scatter_custom_fusion.1 = bf16[3072,256]{1,0:T(8,128)(2,1)} fusion(s32[2048]{0:T(1024)} %bitcast.92, bf16[2048,256]{1,0:T(8,128)(2,1)S(1)} %reshape.359, bf16[]{:T(256)} %constant.43.clone.1), kind=kCustom, calls=%fused_computation.57 | custom fusion | bytes 1573376 | tf_op jit(solution)/shard_map/scatter | solution.py:122
  294.4 10.3 %all-to-all-start.2 = ((bf16[32,96,256]{2,1,0:T(8,128)(2,1)}), bf16[32,96,256]{2,1,0:T(8,128)(2,1)S(1)}, u32[]{:S(2)}, u32[]{:S(2)}) async-start(bf16[32,96,256]{2,1,0:T(8,128)(2,1)} %bitcast.77), calls=%async_computation.3 | async-start | bytes 3145728 | tf_op jit(solution)/shard_map/all_to_all | solution.py:123
  305.4 1.5 pad_maximum_fusion
  307.5 0.7 reduce.6
  308.3 37.0 %all-to-all-done.2 = bf16[32,96,256]{2,1,0:T(8,128)(2,1)S(1)} async-done(((bf16[32,96,256]{2,1,0:T(8,128)(2,1)}), bf16[32,96,256]{2,1,0:T(8,128)(2,1)S(1)}, u32[]{:S(2)}, u32[]{:S(2)}) %all-to-all-start.2) | async-done | bytes 1572896 | tf_op jit(solution)/shard_map/all_to_all | solution.py:123
  345.3 18.1 %scatter_custom_fusion.2 = f32[1024,256]{1,0:T(8,128)} fusion(s32[3072]{0:T(1024)S(1)} %bitcast.95, bf16[3072,256]{1,0:T(8,128)(2,1)S(1)} %bitcast.76, f32[]{:T(128)} %constant.33.clone.1), kind=kCustom, calls=%fused_computation.7 | custom fusion | flops 1572864 | bytes 2621444 | tf_op jit(solution)/shard_map/scatter-add | solution.py:135
  363.5 19.7 %scatter_custom_fusion.3 = f32[1024]{0:T(1024)S(1)} fusion(s32[3072]{0:T(1024)S(1)} %bitcast.96, f32[3072]{0:T(1024)S(1)} %reshape.375, f32[]{:T(128)} %constant.33.clone.1), kind=kCustom, calls=%fused_computation.117 | custom fusion | flops 3072 | bytes 4100 | tf_op jit(solution)/shard_map/scatter-add | solution.py:140
  383.2 32.3 %psum.22 = f32[1024]{0:T(1024)S(1)} all-reduce(f32[1024]{0:T(1024)S(1)} %scatter_custom_fusion.3), channel_id=1, replica_groups=mesh['dp'=16,'table'=32] {'dp'}, use_global_device_ids=true, to_apply=%region_18.19 | all-reduce | flops 1024 | bytes 8192 | tf_op jit(solution)/shard_map/psum | solution.py:142
  415.5 177.9 %all-reduce.5.cloned.1.call-done = f32[2,1024,256]{2,1,0:T(8,128)} async-done(((f32[2,1024,256]{2,1,0:T(8,128)}), f32[2,1024,256]{2,1,0:T(8,128)}) %all-reduce.5.cloned.1.call-update) | async-done | bytes 2097168 | tf_op jit(solution)/shard_map/psum | solution.py:114
  593.4 5.3 multiply_add_fusion
  598.7 140.4 %all-reduce.3.cloned.1.call-done = f32[1024,256]{1,0:T(8,128)} async-done(((f32[1024,256]{1,0:T(8,128)}), f32[1024,256]{1,0:T(8,128)}) %all-reduce.3.cloned.1.call-update) | async-done | bytes 1048592 | tf_op jit(solution)/shard_map/psum | solution.py:142
  739.2 3.5 multiply_add_fusion.1
  (80 shorter events, 7.5 us)
Async XLA Ops:
  7.2 52.5 %copy-start = (bf16[1024,256]{1,0:T(8,128)(2,1)S(1)}, bf16[1024,256]{1,0:T(8,128)(2,1)}, u32[]{:S(2)}) copy-start(bf16[1024,256]{1,0:T(8,128)(2,1)} %param.7) | copy-start | bytes 1572868
  7.2 1.4 copy-start.1
  30.4 48.3 %copy-start.9 = (s32[2048,1]{0,1:T(1,128)}, s32[2048,1]{0,1:T(1,128)S(1)}, u32[]{:S(2)}) copy-start(s32[2048,1]{0,1:T(1,128)S(1)} %compare_select_fusion.2) | copy-start | bytes 24580
  72.2 45.7 %all-to-all-start.1 = ((bf16[32,96,256]{2,1,0:T(8,128)(2,1)}), bf16[32,96,256]{2,1,0:T(8,128)(2,1)S(1)}, u32[]{:S(2)}, u32[]{:S(2)}) async-start(bf16[32,96,256]{2,1,0:T(8,128)(2,1)} %broadcast_select_fusion), calls=%async_computation.1 | async-start | bytes 3145728 | tf_op jit(solution)/shard_map/all_to_all | solution.py:52
  78.6 119.9 %all-gather.2.cloned.1.call-start = ((), (), s32[]{:S(2)}) async-start(), calls=%async_computation.4 | async-start | bytes 1114112 | tf_op jit(solution)/shard_map/all_gather | solution.py:63
  125.8 3.3 copy-start.6
  125.8 4.7 copy-start.4
  128.9 1.9 copy-start.3
  130.1 150.4 %reduce-scatter.2.cloned.1.call-start = ((), (), s32[]{:S(2)}) async-start(), calls=%async_computation.5 | async-start | bytes 2228224 | tf_op jit(solution)/shard_map/reduce_scatter | solution.py:77
  200.6 1.9 copy-start.15
  202.5 1.9 copy-start.2
  202.5 3.7 copy-start.5
  206.2 75.3 %copy-start.7 = (bf16[1024,256]{1,0:T(8,128)(2,1)S(1)}, bf16[1024,256]{1,0:T(8,128)(2,1)}, u32[]{:S(2)}) copy-start(bf16[1024,256]{1,0:T(8,128)(2,1)} %param.11) | copy-start | bytes 1572868
  206.2 76.0 %copy-start.12 = (f32[128]{0:T(128)S(1)}, f32[128]{0:T(128)}, u32[]{:S(2)}) copy-start(f32[128]{0:T(128)} %get-tuple-element.18) | copy-start | bytes 1540
  206.2 76.0 %copy-start.13 = (f32[128]{0:T(128)S(1)}, f32[128]{0:T(128)}, u32[]{:S(2)}) copy-start(f32[128]{0:T(128)} %get-tuple-element.19) | copy-start | bytes 1540
  206.2 76.0 %copy-start.14 = (f32[128]{0:T(128)S(1)}, f32[128]{0:T(128)}, u32[]{:S(2)}) copy-start(f32[128]{0:T(128)} %get-tuple-element.16) | copy-start | bytes 1540
  294.4 50.9 %all-to-all-start.2 = ((bf16[32,96,256]{2,1,0:T(8,128)(2,1)}), bf16[32,96,256]{2,1,0:T(8,128)(2,1)S(1)}, u32[]{:S(2)}, u32[]{:S(2)}) async-start(bf16[32,96,256]{2,1,0:T(8,128)(2,1)} %bitcast.77), calls=%async_computation.3 | async-start | bytes 3145728 | tf_op jit(solution)/shard_map/all_to_all | solution.py:123
  304.7 288.7 %all-reduce.5.cloned.1.call-start = ((), (), s32[]{:S(2)}) async-start(), calls=%async_computation.7 | async-start | bytes 4194304 | tf_op jit(solution)/shard_map/psum | solution.py:114
  306.9 56.6 %copy-start.8 = (f32[32,1,96]{2,0,1:T(8,128)S(1)}, f32[32,1,96]{2,0,1:T(8,128)}, u32[]{:S(2)}) copy-start(f32[32,1,96]{2,0,1:T(8,128)} %get-tuple-element.2) | copy-start | bytes 36868
  306.9 286.5 %copy-start.10 = (s32[2,1024]{1,0:T(2,128)S(1)}, s32[2,1024]{1,0:T(2,128)}, u32[]{:S(2)}) copy-start(s32[2,1024]{1,0:T(2,128)} %param.13) | copy-start | bytes 24580
  306.9 432.2 %all-reduce.3.cloned.1.call-start = ((), (), s32[]{:S(2)}) async-start(), calls=%async_computation.6 | async-start | bytes 2097152 | tf_op jit(solution)/shard_map/psum | solution.py:142
  593.4 145.7 %copy-start.11 = (s32[1024]{0:T(1024)S(1)}, s32[1024]{0:T(1024)}, u32[]{:S(2)}) copy-start(s32[1024]{0:T(1024)} %param.12) | copy-start | bytes 12292
Sparse Core Ops, SparseCore 0:
  130.2 68.2 all-gather.1
  202.7 77.8 reduce-scatter.1
  311.0 282.3 all-reduce.4
  597.0 142.0 all-reduce.2
where the time goes:
time: 750 us; the launch traced here: 749 us
  waiting for transfers between devices  536 us (71%)
  other arithmetic  66.8 us (9%)
  local copies, waits for them, and re-layouts  54.5 us (7%)
  blocking collectives  52.7 us (7%)
  starting transfers between devices  17.1 us (2%)
  between operations  14.2 us (2%)
  matrix products  8.08 us (1%)
    psum x1, waiting for transfers between devices, body(): tower_sum = lax.psum(tower_part, ('dp', 'table'))  178 us
    psum x1, waiting for transfers between devices, body(): row_sum, row_count = lax.psum((row_sum, row_count), 'dp')  140 us
    reduce_scatter x1, waiting for transfers between devices, body(): lax.psum_scatter(lax.dot_general(probs, query_vec, (((0,), (0,)), ((), ()...  73.6 us
    all_gather x1, waiting for transfers between devices, body(): all_items = lax.all_gather(item_vec, 'dp', axis=0, tiled=True)  67.7 us
    all_to_all x1, waiting for transfers between devices, body(): lax.all_to_all(fetched, 'table', split_axis=0, concat_axis=0, tiled=True)  39.2 us
    all_to_all x1, waiting for transfers between devices, body(): lax.all_to_all(grad_out.reshape(shards, capacity, emb_width), 'table', sp...  37 us
    psum x1, blocking collectives, body(): row_sum, row_count = lax.psum((row_sum, row_count), 'dp')  32.3 us
    all_to_all x1, blocking collectives, body(): lax.all_to_all(outgoing, 'table', split_axis=0, concat_axis=0, tiled=True)  20.4 us
  transfers between devices with their start and end apart: 6, of which 6 were waited for; matrix products, arithmetic and copies ran while one was open for 7% of the time, Pallas kernels for 0%

commit v1 on v0

--- a/solution.py
+++ b/solution.py
@@ -111,7 +111,7 @@
             ),
         ]
     )
-    tower_sum = lax.psum(tower_part, ("dp", "table"))
+    tower_sum = lax.psum(lax.psum(tower_part, "dp"), "table")
     back_all = jnp.concatenate(
         [query_back.reshape(batch, feats, emb_width), item_back.reshape(batch, feats, emb_width)],
         axis=1,

time: 750 us -> 821 us (1.095)
  the two profiles are of different devices: /device:TPU:4 before, /device:TPU:1 now
where the time goes in v1:
time: 821 us; the launch traced here: 820 us
  waiting for transfers between devices  601 us (73%)
  other arithmetic  65.8 us (8%)
  local copies, waits for them, and re-layouts  54.5 us (7%)
  blocking collectives  50.4 us (6%)
  starting transfers between devices  26 us (3%)
  between operations  14.2 us (2%)
    psum x1, waiting for transfers between devices, body(): tower_sum = lax.psum(lax.psum(tower_part, 'dp'), 'table')  234 us
    psum x1, waiting for transfers between devices, body(): row_sum, row_count = lax.psum((row_sum, row_count), 'dp')  162 us
    reduce_scatter x1, waiting for transfers between devices, body(): lax.psum_scatter(lax.dot_general(probs, query_vec, (((0,), (0,)), ((), ()...  72.4 us
    all_gather x1, waiting for transfers between devices, body(): all_items = lax.all_gather(item_vec, 'dp', axis=0, tiled=True)  58 us
    all_to_all x1, waiting for transfers between devices, body(): lax.all_to_all(fetched, 'table', split_axis=0, concat_axis=0, tiled=True)  39.1 us
    all_to_all x1, waiting for transfers between devices, body(): lax.all_to_all(grad_out.reshape(shards, capacity, emb_width), 'table', sp...  35.6 us
    psum x1, blocking collectives, body(): row_sum, row_count = lax.psum((row_sum, row_count), 'dp')  26.8 us
    all_to_all x1, blocking collectives, body(): lax.all_to_all(outgoing, 'table', split_axis=0, concat_axis=0, tiled=True)  23.6 us
  transfers between devices with their start and end apart: 6, of which 6 were waited for; matrix products, arithmetic and copies ran while one was open for 4% of the time, Pallas kernels for 0%

profile of v1, /device:TPU:1, one launch (start us, length us, event | category | flops | bytes accessed | tf_op | source)
XLA Modules:
  0.0 820.1 jit_solution(12416371590583594255)
XLA Ops:
  7.2 1.0 copy.37
  8.6 11.8 %gather_fusion = s32[2048]{0:T(1024)S(1)} fusion(s32[32768]{0:T(1024)S(1)} %copy-done.1, s32[2048]{0:T(1024)S(1)} %broadcast_clamp_fusion.2), kind=kCustom, calls=%fused_computation | custom fusion | bytes 24576 | tf_op jit(solution)/shard_map/gather | solution.py:40
  20.4 9.1 %reduce-window.6 = s32[32,16,128]{2,1,0:T(8,128)S(1)} reduce-window(s32[32,16,128]{2,1,0:T(8,128)S(1)} %fusion.35, s32[]{:T(128)} %constant.35.clone.1), window={size=1x1x128 pad=0_0x0_0x127_0}, to_apply=%region_0.1 | reduce-window | flops 8323072 | bytes 524292 | tf_op jit(solution)/shard_map/reduce-window
  30.4 8.1 scatter_custom_fusion
  38.6 23.6 %all_to_all.22 = s32[32,1,96]{2,1,0:T(1,128)S(1)} all-to-all(s32[32,1,96]{2,1,0:T(1,128)S(1)} %all_to_all.14), channel_id=1, replica_groups=mesh['dp'=16,'table'=32] {'table'}, dimensions={0} | all-to-all | bytes 24576 | tf_op jit(solution)/shard_map/all_to_all | solution.py:48
  62.9 11.1 %gather_fusion.1 = bf16[3072,256]{1,0:T(8,128)(2,1)S(1)} fusion(bf16[1024,256]{1,0:T(8,128)(2,1)S(1)} %copy-done, s32[3072]{0:T(1024)S(1)} %broadcast_clamp_fusion), kind=kCustom, calls=%fused_computation.1 | custom fusion | bytes 3158016 | tf_op jit(solution)/shard_map/gather | solution.py:50
  73.9 1.5 broadcast_select_fusion
  75.4 4.2 all-to-all-start.1
  79.7 39.1 %all-to-all-done.1 = bf16[32,96,256]{2,1,0:T(8,128)(2,1)S(1)} async-done(((bf16[32,96,256]{2,1,0:T(8,128)(2,1)}), bf16[32,96,256]{2,1,0:T(8,128)(2,1)S(1)}, u32[]{:S(2)}, u32[]{:S(2)}) %all-to-all-start.1) | async-done | bytes 1572896 | tf_op jit(solution)/shard_map/all_to_all | solution.py:52
  118.8 7.5 gather_fusion.2
  126.8 2.8 reduce_sum.88
  130.1 0.9 convolution_convert_fusion
  131.7 58.0 %all-gather.2.cloned.1.call-done = bf16[2048,256]{1,0:T(8,128)(2,1)} async-done(((bf16[128,256]{1,0:T(8,128)(2,1)}), bf16[2048,256]{1,0:T(8,128)(2,1)}) %all-gather.2.cloned.1.call-update) | async-done | bytes 1048592 | tf_op jit(solution)/shard_map/all_gather | solution.py:63
  189.7 1.8 fusion.56
  191.8 1.9 fusion.53
  193.8 1.8 multiply_reduce_fusion.2
  195.6 1.8 fusion.36
  198.1 72.4 %reduce-scatter.2.cloned.1.call-done = f32[128,256]{1,0:T(8,128)} async-done(((f32[2048,256]{1,0:T(8,128)}), f32[128,256]{1,0:T(8,128)}) %reduce-scatter.2.cloned.1.call-update) | async-done | bytes 131088 | tf_op jit(solution)/shard_map/reduce_scatter | solution.py:77
  270.5 1.0 fusion.38
  272.5 0.7 broadcast_in_dim.40
  273.6 10.7 %scatter_custom_fusion.1 = bf16[3072,256]{1,0:T(8,128)(2,1)} fusion(s32[2048]{0:T(1024)} %bitcast.92, bf16[2048,256]{1,0:T(8,128)(2,1)S(1)} %reshape.359, bf16[]{:T(256)} %constant.43.clone.1), kind=kCustom, calls=%fused_computation.57 | custom fusion | bytes 1573376 | tf_op jit(solution)/shard_map/scatter | solution.py:122
  284.4 21.4 %all-to-all-start.2 = ((bf16[32,96,256]{2,1,0:T(8,128)(2,1)}), bf16[32,96,256]{2,1,0:T(8,128)(2,1)S(1)}, u32[]{:S(2)}, u32[]{:S(2)}) async-start(bf16[32,96,256]{2,1,0:T(8,128)(2,1)} %bitcast.77), calls=%async_computation.3 | async-start | bytes 3145728 | tf_op jit(solution)/shard_map/all_to_all | solution.py:123
  306.3 0.7 reduce.6
  307.9 1.5 pad_maximum_fusion
  309.3 35.6 %all-to-all-done.2 = bf16[32,96,256]{2,1,0:T(8,128)(2,1)S(1)} async-done(((bf16[32,96,256]{2,1,0:T(8,128)(2,1)}), bf16[32,96,256]{2,1,0:T(8,128)(2,1)S(1)}, u32[]{:S(2)}, u32[]{:S(2)}) %all-to-all-start.2) | async-done | bytes 1572896 | tf_op jit(solution)/shard_map/all_to_all | solution.py:123
  345.0 18.1 %scatter_custom_fusion.2 = f32[1024,256]{1,0:T(8,128)} fusion(s32[3072]{0:T(1024)S(1)} %bitcast.95, bf16[3072,256]{1,0:T(8,128)(2,1)S(1)} %bitcast.76, f32[]{:T(128)} %constant.33.clone.1), kind=kCustom, calls=%fused_computation.7 | custom fusion | flops 1572864 | bytes 2621444 | tf_op jit(solution)/shard_map/scatter-add | solution.py:135
  363.2 161.5 %all-reduce.6.cloned.1.call-done = (f32[1024,256]{1,0:T(8,128)}, f32[2,1024,256]{2,1,0:T(8,128)}) async-done(((f32[1024,256]{1,0:T(8,128)}, f32[2,1024,256]{2,1,0:T(8,128)}), (f32[1024,256]{1,0:T(8,128)}, f32[2,1024,256]{2,1,0:T(8,128)})) %all-reduce.6.cloned.1.call-update) | async-done | bytes 3145744 | tf_op jit(solution)/shard_map/psum | solution.py:142
  524.8 19.7 %scatter_custom_fusion.3 = f32[1024]{0:T(1024)S(1)} fusion(s32[3072]{0:T(1024)S(1)} %bitcast.96, f32[3072]{0:T(1024)S(1)} %reshape.375, f32[]{:T(128)} %constant.33.clone.1), kind=kCustom, calls=%fused_computation.117 | custom fusion | flops 3072 | bytes 4100 | tf_op jit(solution)/shard_map/scatter-add | solution.py:140
  544.5 26.8 %psum.29 = f32[1024]{0:T(1024)S(1)} all-reduce(f32[1024]{0:T(1024)S(1)} %scatter_custom_fusion.3), channel_id=1, replica_groups=mesh['dp'=16,'table'=32] {'dp'}, use_global_device_ids=true, to_apply=%region_18.19 | all-reduce | flops 1024 | bytes 8192 | tf_op jit(solution)/shard_map/psum | solution.py:142
  571.4 2.5 multiply_add_fusion.1
  573.9 234.4 %all-reduce.4.cloned.1.call-done = f32[2,1024,256]{2,1,0:T(8,128)} async-done(((f32[2,1024,256]{2,1,0:T(8,128)}), f32[2,1024,256]{2,1,0:T(8,128)}) %all-reduce.4.cloned.1.call-update) | async-done | bytes 2097168 | tf_op jit(solution)/shard_map/psum | solution.py:114
  808.3 5.3 multiply_add_fusion
  (82 shorter events, 7.5 us)
Async XLA Ops:
  7.2 55.7 %copy-start = (bf16[1024,256]{1,0:T(8,128)(2,1)S(1)}, bf16[1024,256]{1,0:T(8,128)(2,1)}, u32[]{:S(2)}) copy-start(bf16[1024,256]{1,0:T(8,128)(2,1)} %param.7) | copy-start | bytes 1572868
  7.2 1.4 copy-start.1
  30.4 49.3 %copy-start.10 = (s32[2048,1]{0,1:T(1,128)}, s32[2048,1]{0,1:T(1,128)S(1)}, u32[]{:S(2)}) copy-start(s32[2048,1]{0,1:T(1,128)S(1)} %compare_select_fusion.2) | copy-start | bytes 24580
  75.4 43.4 %all-to-all-start.1 = ((bf16[32,96,256]{2,1,0:T(8,128)(2,1)}), bf16[32,96,256]{2,1,0:T(8,128)(2,1)S(1)}, u32[]{:S(2)}, u32[]{:S(2)}) async-start(bf16[32,96,256]{2,1,0:T(8,128)(2,1)} %broadcast_select_fusion), calls=%async_computation.1 | async-start | bytes 3145728 | tf_op jit(solution)/shard_map/all_to_all | solution.py:52
  79.6 110.1 %all-gather.2.cloned.1.call-start = ((), (), s32[]{:S(2)}) async-start(), calls=%async_computation.4 | async-start | bytes 1114112 | tf_op jit(solution)/shard_map/all_gather | solution.py:63
  126.7 3.3 copy-start.6
  126.8 4.7 copy-start.4
  129.8 1.9 copy-start.3
  131.0 139.5 %reduce-scatter.2.cloned.1.call-start = ((), (), s32[]{:S(2)}) async-start(), calls=%async_computation.5 | async-start | bytes 2228224 | tf_op jit(solution)/shard_map/reduce_scatter | solution.py:77
  191.8 1.9 copy-start.16
  193.7 1.9 copy-start.2
  193.7 3.7 copy-start.5
  197.4 74.1 %copy-start.7 = (bf16[1024,256]{1,0:T(8,128)(2,1)S(1)}, bf16[1024,256]{1,0:T(8,128)(2,1)}, u32[]{:S(2)}) copy-start(bf16[1024,256]{1,0:T(8,128)(2,1)} %param.11) | copy-start | bytes 1572868
  197.4 74.8 %copy-start.13 = (f32[128]{0:T(128)S(1)}, f32[128]{0:T(128)}, u32[]{:S(2)}) copy-start(f32[128]{0:T(128)} %get-tuple-element.20) | copy-start | bytes 1540
  197.4 74.8 %copy-start.14 = (f32[128]{0:T(128)S(1)}, f32[128]{0:T(128)}, u32[]{:S(2)}) copy-start(f32[128]{0:T(128)} %get-tuple-element.21) | copy-start | bytes 1540
  197.4 74.8 %copy-start.15 = (f32[128]{0:T(128)S(1)}, f32[128]{0:T(128)}, u32[]{:S(2)}) copy-start(f32[128]{0:T(128)} %get-tuple-element.18) | copy-start | bytes 1540
  284.4 60.6 %all-to-all-start.2 = ((bf16[32,96,256]{2,1,0:T(8,128)(2,1)}), bf16[32,96,256]{2,1,0:T(8,128)(2,1)S(1)}, u32[]{:S(2)}, u32[]{:S(2)}) async-start(bf16[32,96,256]{2,1,0:T(8,128)(2,1)} %bitcast.77), calls=%async_computation.3 | async-start | bytes 3145728 | tf_op jit(solution)/shard_map/all_to_all | solution.py:123
  305.8 218.9 %all-reduce.6.cloned.1.call-start = ((), (), s32[]{:S(2)}) async-start(), calls=%async_computation.7 | async-start | bytes 6291456 | tf_op jit(solution)/shard_map/psum | solution.py:142
  363.1 161.6 %copy-start.9 = (f32[32,1,96]{2,0,1:T(8,128)S(1)}, f32[32,1,96]{2,0,1:T(8,128)}, u32[]{:S(2)}) copy-start(f32[32,1,96]{2,0,1:T(8,128)} %get-tuple-element.4) | copy-start | bytes 36868
  363.1 208.3 %copy-start.12 = (s32[1024]{0:T(1024)S(1)}, s32[1024]{0:T(1024)}, u32[]{:S(2)}) copy-start(s32[1024]{0:T(1024)} %param.12) | copy-start | bytes 12292
  363.1 445.2 %all-reduce.4.cloned.1.call-start = ((), (), s32[]{:S(2)}) async-start(), calls=%async_computation.6 | async-start | bytes 4194304 | tf_op jit(solution)/shard_map/psum | solution.py:114
  524.7 46.7 %copy-start.8 = (f32[1024,256]{1,0:T(8,128)S(1)}, f32[1024,256]{1,0:T(8,128)}, u32[]{:S(2)}) copy-start(f32[1024,256]{1,0:T(8,128)} %get-tuple-element.2) | copy-start | bytes 3145732
  524.7 283.6 %copy-start.11 = (s32[2,1024]{1,0:T(2,128)S(1)}, s32[2,1024]{1,0:T(2,128)}, u32[]{:S(2)}) copy-start(s32[2,1024]{1,0:T(2,128)} %param.13) | copy-start | bytes 24580
Sparse Core Ops, SparseCore 0:
  131.1 58.5 all-gather.1
  193.9 76.5 reduce-scatter.1
  363.2 161.3 all-reduce.5
  527.4 280.8 all-reduce.3
